TPU v7x, 128 devices: a whole 4x4x4 slice. The times are simulated.
128 devices in a mesh: seq: 16 (over x, y), chan: 8 (over z, core).
Axes of the slice: x: 4, y: 4, z: 4, core: 2. Of those that a mesh axis runs over, the one named last changes fastest.
Arguments:
- hyena_query: bfloat16 [4096, 8192], P('seq', 'chan'), may hold values from -6 to 6
- hyena_key: bfloat16 [4096, 8192], P('seq', 'chan'), may hold values from -6 to 6
- hyena_value: bfloat16 [4096, 8192], P('seq', 'chan'), may hold values from -6 to 6
- bias: float32 [8192], P('chan'), may hold values from 0.5 to 1.5
- groups: int32 [8192], P('chan'), may hold values from 0 to 511
- filters: float32 [512, 4096], P('chan', 'seq'), may hold values from -1.5 to 1.5
- att_queries: bfloat16 [4096, 8192], P('seq', 'chan'), may hold values from -45 to 45
- att_keys: bfloat16 [4096, 8192], P('seq', 'chan'), may hold values from -5 to 5
- block_mask: int32 [32, 32], P('seq'), may hold values from 0 to 1, as said below
Outputs:
- hyena_out: bfloat16 [4096, 8192], P('seq', 'chan')
- attn_out: bfloat16 [4096, 8192], P('seq', 'chan')
Inputs may be any that keep to these rules, and one draw needn't show every extreme that they name: block_mask[i, i] = 1 and block_mask[i, j] = 0 for j > i.
All inputs are finite; a program needn't handle non-finite values.
Results may differ from a plain program's by a relative error of at most 0.014.
Values may be sent and summed in bfloat16 or wider, within the bound.
No kernel may reach another device: no remote copies, remote signals or barrier semaphores. Data moves between devices by JAX's collectives and lax.ppermute only.
A program may use at most 128 MiB of HBM per device.

v0:
```python
import math
import jax
import jax.numpy as jnp
from jax import lax
from jax.sharding import PartitionSpec as P

HD = 128
ABLK = 128
highest = lax.Precision.HIGHEST


def swapped(value, axis, stride):
    mask = 2**stride
    pairs = [(source, source ^ mask) for source in range(lax.axis_size(axis))]
    return lax.ppermute(value, axis, pairs)


def shortened(x):

    def short(part):
        return part.astype(jnp.bfloat16) if part.dtype == jnp.float32 else part

    return jax.tree.map(short, x)


def unit_angle(numer, denom):
    return 2.0 * math.pi / denom * numer.astype(jnp.float32)


def twist(real_part, imag_part, cosine, sine):
    return (real_part * cosine - imag_part * sine, real_part * sine + imag_part * cosine)


def expand_pair(signal, device, rows_dev, length):
    positions = device * rows_dev + jnp.arange(rows_dev, dtype=jnp.int32)
    angles = math.pi / length * positions.astype(jnp.float32)
    values = signal.astype(jnp.float32)
    cosine = jnp.cos(angles)[:, None]
    sine = jnp.sin(angles)[:, None]
    real_part = jnp.stack([values, values * cosine])
    imag_part = jnp.stack([jnp.zeros_like(values), -values * sine])
    return (real_part, imag_part)


def section_twiddle(device, level, rows_dev, sign):
    inner = device % (1 << level) * rows_dev + jnp.arange(rows_dev, dtype=jnp.int32)
    angles = unit_angle(inner, rows_dev << level + 1)
    return (jnp.cos(angles)[:, None], sign * jnp.sin(angles)[:, None])


def forward_section(current, partner, device, level, rows_dev):
    cosine, sine = section_twiddle(device, level, rows_dev, -1.0)
    upper = device >> level & 1 == 1
    diff_re = partner[0] - current[0]
    diff_im = partner[1] - current[1]
    turned_re, turned_im = twist(diff_re, diff_im, cosine, sine)
    return (
        jnp.where(upper, turned_re, current[0] + partner[0]),
        jnp.where(upper, turned_im, current[1] + partner[1]),
    )


def inverse_section(current, partner, device, level, rows_dev):
    cosine, sine = section_twiddle(device, level, rows_dev, 1.0)
    upper = device >> level & 1 == 1
    moved_re = jnp.where(upper, current[0], partner[0])
    moved_im = jnp.where(upper, current[1], partner[1])
    base_re = jnp.where(upper, partner[0], current[0])
    base_im = jnp.where(upper, partner[1], current[1])
    turned_re, turned_im = twist(moved_re, moved_im, cosine, sine)
    factor = jnp.where(upper, -1.0, 1.0)
    return (base_re + factor * turned_re, base_im + factor * turned_im)


def local_dft(real_part, imag_part, rows_dev, sign):
    index = jnp.arange(rows_dev, dtype=jnp.int32)
    angles = unit_angle(index[:, None] * index[None, :] % rows_dev, rows_dev)
    cosine = jnp.cos(angles)
    sine = sign * jnp.sin(angles)

    def apply_matrix(matrix, data):
        return jnp.einsum("km,emc->ekc", matrix, data, precision=highest)

    new_re = apply_matrix(cosine, real_part) - apply_matrix(sine, imag_part)
    new_im = apply_matrix(cosine, imag_part) + apply_matrix(sine, real_part)
    return (new_re, new_im)


def butterfly_conv(mixed, bank, groups):
    rows_dev, channels = mixed.shape
    devices = lax.axis_size("seq")
    length = rows_dev * devices
    bit_count = devices.bit_length() - 1
    device = lax.axis_index("seq")
    top_level = bit_count - 1
    partner_mixed = swapped(mixed, "seq", top_level)
    current = expand_pair(mixed, device, rows_dev, length)
    partner = expand_pair(partner_mixed, jnp.bitwise_xor(device, 1 << top_level), rows_dev, length)
    state = forward_section(current, partner, device, top_level, rows_dev)
    for level in range(top_level - 1, -1, -1):
        received = swapped(shortened(jnp.stack(state)), "seq", level)
        state = forward_section(state, (received[0], received[1]), device, level, rows_dev)
    spec_re, spec_im = local_dft(state[0], state[1], rows_dev, -1.0)
    residue = jnp.zeros((), jnp.int32)
    for level in range(bit_count):
        residue = residue + ((device >> level & 1) << bit_count - 1 - level)
    freq_even = 2 * (residue + devices * jnp.arange(rows_dev, dtype=jnp.int32))
    freqs = jnp.concatenate([freq_even, freq_even + 1])
    lags = jnp.arange(length, dtype=jnp.int32)
    angles = unit_angle(lags[:, None] * freqs[None, :] % (2 * length), 2 * length)
    table_re = jnp.dot(bank, jnp.cos(angles), precision=highest)
    table_im = -jnp.dot(bank, jnp.sin(angles), precision=highest)
    chosen_re = jnp.take(table_re, groups, axis=0).T.reshape(2, rows_dev, channels)
    chosen_im = jnp.take(table_im, groups, axis=0).T.reshape(2, rows_dev, channels)
    prod_re, prod_im = twist(spec_re, spec_im, chosen_re, chosen_im)
    state = local_dft(prod_re, prod_im, rows_dev, 1.0)
    for level in range(bit_count):
        received = swapped(shortened(jnp.stack(state)), "seq", level)
        state = inverse_section(state, (received[0], received[1]), device, level, rows_dev)
    positions = device * rows_dev + jnp.arange(rows_dev, dtype=jnp.int32)
    final_angles = math.pi / length * positions.astype(jnp.float32)
    cosine = jnp.cos(final_angles)[:, None]
    sine = jnp.sin(final_angles)[:, None]
    return (state[0][0] + cosine * state[0][1] - sine * state[1][1]) / (2.0 * length)


def attention(att_queries, att_keys, hyena_out, block_mask):
    rows_dev, channels = att_queries.shape
    head_count = channels // HD
    device = lax.axis_index("seq")
    block_count = block_mask.shape[1]
    queries = att_queries.reshape(rows_dev, head_count, HD)
    mask_rows = jnp.repeat(block_mask, ABLK, axis=0).astype(jnp.float32)
    query_pos = device * rows_dev + jnp.arange(rows_dev, dtype=jnp.int32)
    scale = HD ** (-0.5)
    key_piece = lax.all_gather(att_keys, "seq", axis=0, tiled=True)
    value_piece = lax.all_gather(hyena_out, "seq", axis=0, tiled=True)
    piece_rows = key_piece.shape[0]
    key_pos = jnp.arange(piece_rows, dtype=jnp.int32)
    onehot = (
        jnp.arange(block_count, dtype=jnp.int32)[:, None] == (key_pos // ABLK)[None, :]
    ).astype(jnp.float32)
    allowed = (jnp.dot(mask_rows, onehot, preferred_element_type=jnp.float32) > 0.5) & (
        key_pos[None, :] <= query_pos[:, None]
    )
    keys_here = key_piece.reshape(piece_rows, head_count, HD)
    values_here = value_piece.reshape(piece_rows, head_count, HD)
    scores = (
        jnp.einsum("thd,shd->hts", queries, keys_here, preferred_element_type=jnp.float32) * scale
    )
    scores = jnp.where(allowed[None], scores, -1e30)
    old_max = jnp.full((head_count, rows_dev), -1e30, jnp.float32)
    new_max = jnp.maximum(old_max, jnp.max(scores, axis=-1))
    weights = jnp.where(allowed[None], jnp.exp(scores - new_max[..., None]), 0.0)
    new_total = jnp.sum(weights, axis=-1)
    new_acc = jnp.einsum(
        "hts,shd->htd",
        weights.astype(jnp.bfloat16),
        values_here,
        preferred_element_type=jnp.float32,
    )
    result = new_acc / new_total[..., None]
    return result.transpose(1, 0, 2).reshape(rows_dev, channels).astype(jnp.bfloat16)


def on_device(
    hyena_query, hyena_key, hyena_value, bias, groups, filters, att_queries, att_keys, block_mask
):
    mixed = (hyena_key.astype(jnp.float32) * hyena_value.astype(jnp.float32)).astype(jnp.bfloat16)
    bank = lax.all_gather(filters.astype(jnp.bfloat16), "chan", axis=0, tiled=True).astype(
        filters.dtype
    )
    bank = lax.all_gather(bank.astype(jnp.bfloat16), "seq", axis=1, tiled=True).astype(bank.dtype)
    conv = butterfly_conv(mixed, bank, groups)
    hyena_out = (
        hyena_query.astype(jnp.float32) * (conv + bias[None, :] * mixed.astype(jnp.float32))
    ).astype(jnp.bfloat16)
    attn_out = attention(att_queries, att_keys, hyena_out, block_mask)
    return (hyena_out, attn_out)


def solution(mesh):
    return jax.shard_map(
        on_device,
        mesh=mesh,
        in_specs=(
            P("seq", "chan"),
            P("seq", "chan"),
            P("seq", "chan"),
            P("chan"),
            P("chan"),
            P("chan", "seq"),
            P("seq", "chan"),
            P("seq", "chan"),
            P("seq", None),
        ),
        out_specs=(P("seq", "chan"), P("seq", "chan")),
        check_vma=False,
    )
```

profile of v0, /device:TPU:0, one launch (start us, length us, event | category | flops | bytes accessed | tf_op | source)
XLA Modules:
  0.0 675.8 jit_solution(9191021837587464185)
XLA Ops:
  8.1 15.2 %all_gather.12 = bf16[512,256]{1,0:T(8,128)(2,1)} all-gather(bf16[64,256]{1,0:T(8,128)(2,1)S(1)} %convert_element_type.294), channel_id=1, replica_groups=mesh['seq'=16,'chan'=8] {'chan'}, dimensions={0}, use_global_device_ids=true | all-gather | bytes 294912 | tf_op jit(solution)/shard_map/all_gather | solution.py:170
  27.2 3.0 collective-permute-start
  30.5 14.4 %collective-permute-done = bf16[256,1024]{0,1:T(8,128)(2,1)S(1)} collective-permute-done((bf16[256,1024]{0,1:T(8,128)(2,1)S(1)}, bf16[256,1024]{0,1:T(8,128)(2,1)S(1)}, u32[]{:S(2)}, u32[]{:S(2)}) %collective-permute-start) | collective-permute-done | bytes 524320 | tf_op jit(solution)/shard_map/ppermute | solution.py:15
  45.2 2.2 convert_bitcast_fusion.12
  47.4 1.6 pad_maximum_fusion.2
  49.0 2.0 collective-permute-start.1
  51.0 62.4 %collective-permute-done.1 = bf16[2,2,256,1024]{2,3,1,0:T(8,128)(2,1)} collective-permute-done((bf16[2,2,256,1024]{2,3,1,0:T(8,128)(2,1)}, bf16[2,2,256,1024]{2,3,1,0:T(8,128)(2,1)}, u32[]{:S(2)}, u32[]{:S(2)}) %collective-permute-start.1) | collective-permute-done | bytes 2097184 | tf_op jit(solution)/shard_map/ppermute | solution.py:15
  113.4 5.3 convert_bitcast_fusion.10
  118.9 2.7 collective-permute-start.2
  121.6 45.3 %collective-permute-done.2 = bf16[2,2,256,1024]{2,3,1,0:T(8,128)(2,1)} collective-permute-done((bf16[2,2,256,1024]{2,3,1,0:T(8,128)(2,1)S(1)}, bf16[2,2,256,1024]{2,3,1,0:T(8,128)(2,1)}, u32[]{:S(2)}, u32[]{:S(2)}) %collective-permute-start.2) | collective-permute-done | bytes 2097184 | tf_op jit(solution)/shard_map/ppermute | solution.py:15
  166.9 5.3 convert_bitcast_fusion.8
  173.7 2.0 copy.32
  176.1 62.9 %collective-permute-done.3 = bf16[2,2,256,1024]{2,3,1,0:T(8,128)(2,1)} collective-permute-done((bf16[2,2,256,1024]{2,3,1,0:T(8,128)(2,1)}, bf16[2,2,256,1024]{2,3,1,0:T(8,128)(2,1)}, u32[]{:S(2)}, u32[]{:S(2)}) %collective-permute-start.3) | collective-permute-done | bytes 2097184 | tf_op jit(solution)/shard_map/ppermute | solution.py:15
  239.1 3.2 fusion.26
  242.3 2.8 fusion.84
  245.2 4.2 fusion.82
  249.4 4.2 convolution_subtract_fusion.1
  253.6 48.3 %fusion.37 = f32[512,512]{0,1:T(8,128)S(1)} fusion(bf16[512,4096]{1,0:T(8,128)(2,1)} %all-gather.4.cloned.1.call-done, s32[512]{0:T(512)S(1)} %pad_add_fusion.1), kind=kOutput, calls=%fused_computation.100 | convolution fusion | flops 12914262016 | bytes 5244928 | tf_op jit(solution)/shard_map/dot_general | solution.py:111
  302.2 49.3 %fusion.46 = f32[512,512]{0,1:T(8,128)} fusion(bf16[512,4096]{1,0:T(8,128)(2,1)} %all-gather.4.cloned.1.call-done, s32[512]{0:T(512)S(1)} %pad_add_fusion.1), kind=kOutput, calls=%fused_computation.103 | convolution fusion | flops 12914524160 | bytes 5244928 | tf_op jit(solution)/shard_map/dot_general | solution.py:112
  351.5 1.6 copy.26
  353.1 4.9 gather_fusion.1
  358.0 4.9 gather_fusion
  362.9 4.0 select_bitcast_fusion
  366.8 2.9 copy.27
  369.7 2.9 copy.28
  372.7 1.9 copy.24
  374.5 3.2 copy.25
  377.8 6.5 fusion.34
  384.3 2.8 fusion.86
  387.1 2.9 convolution_add_fusion
  390.1 2.8 fusion.88
  393.0 3.1 convolution_subtract_fusion
  399.2 39.0 %collective-permute-done.4 = bf16[2,2,256,1024]{2,3,1,0:T(8,128)(2,1)} collective-permute-done((bf16[2,2,256,1024]{2,3,1,0:T(8,128)(2,1)}, bf16[2,2,256,1024]{2,3,1,0:T(8,128)(2,1)}, u32[]{:S(2)}, u32[]{:S(2)}) %collective-permute-start.4) | collective-permute-done | bytes 2097184 | tf_op jit(solution)/shard_map/ppermute | solution.py:15
  438.1 5.5 convert_bitcast_fusion.7
  443.6 1.6 pad_maximum_fusion.6
  445.2 39.0 %collective-permute-done.5 = bf16[2,2,256,1024]{2,3,1,0:T(8,128)(2,1)} collective-permute-done((bf16[2,2,256,1024]{2,3,1,0:T(8,128)(2,1)}, bf16[2,2,256,1024]{2,3,1,0:T(8,128)(2,1)}, u32[]{:S(2)}, u32[]{:S(2)}) %collective-permute-start.5) | collective-permute-done | bytes 2097184 | tf_op jit(solution)/shard_map/ppermute | solution.py:15
  484.3 5.4 convert_bitcast_fusion.5
  490.0 39.7 %collective-permute-done.6 = bf16[2,2,256,1024]{2,3,1,0:T(8,128)(2,1)} collective-permute-done((bf16[2,2,256,1024]{2,3,1,0:T(8,128)(2,1)S(1)}, bf16[2,2,256,1024]{2,3,1,0:T(8,128)(2,1)}, u32[]{:S(2)}, u32[]{:S(2)}) %collective-permute-start.6) | collective-permute-done | bytes 2097184 | tf_op jit(solution)/shard_map/ppermute | solution.py:15
  529.7 5.4 convert_bitcast_fusion.3
  535.1 1.6 pad_maximum_fusion.8
  536.7 2.0 copy.20
  538.7 31.9 %collective-permute-done.7 = bf16[2,2,256,1024]{2,3,1,0:T(8,128)(2,1)} collective-permute-done((bf16[2,2,256,1024]{2,3,1,0:T(8,128)(2,1)}, bf16[2,2,256,1024]{2,3,1,0:T(8,128)(2,1)}, u32[]{:S(2)}, u32[]{:S(2)}) %collective-permute-start.7) | collective-permute-done | bytes 2097184 | tf_op jit(solution)/shard_map/ppermute | solution.py:15
  572.1 2.4 fusion.33
  577.3 2.7 copy.31
  580.0 18.4 %fusion = (f32[8,256]{1,0:T(8,128)S(1)}, f32[8,256,4096]{2,1,0:T(8,128)}) fusion(pred[256,4096]{1,0:T(8,128)(4,1)S(1)} %copy.31, bf16[4096,8,128]{0,2,1:T(8,128)(2,1)} %bitcast.287, bf16[256,1024]{1,0:T(8,128)(2,1)S(1)} %copy-done), kind=kOutput, calls=%fused_computation.4 | convolution fusion | flops 2172647424 | bytes 43524096 | tf_op jit(solution)/shard_map/thd,shd->hts/dot_general | solution.py:149
  598.4 16.4 %fusion.1 = f32[8,256]{1,0:T(8,128)S(1)} fusion(f32[8,256,4096]{2,1,0:T(8,128)} %get-tuple-element.57, f32[8,256]{1,0:T(8,128)S(1)} %broadcast_maximum_fusion, pred[256,4096]{1,0:T(8,128)(4,1)S(1)} %copy.31), kind=kLoop, calls=%fused_computation.5 | loop fusion | flops 41940992 | bytes 34619392 | tf_op jit(solution)/shard_map/reduce_sum | solution.py:155
  615.9 35.7 %all-gather.8.cloned.1.call-done = bf16[4096,1024]{0,1:T(8,128)(2,1)} async-done(((bf16[256,1024]{0,1:T(8,128)(2,1)}), bf16[4096,1024]{0,1:T(8,128)(2,1)}) %all-gather.8.cloned.1.call-update) | async-done | bytes 8388624 | tf_op jit(solution)/shard_map/all_gather | solution.py:137
  651.6 16.3 %divide_convert_fusion = bf16[256,8,128]{0,2,1:T(8,128)(2,1)S(1)} fusion(bf16[4096,8,128]{0,2,1:T(8,128)(2,1)} %bitcast.293, f32[8,256,4096]{2,1,0:T(8,128)} %get-tuple-element.57, f32[8,256]{1,0:T(8,128)S(1)} %broadcast_maximum_fusion, pred[256,4096]{1,0:T(8,128)(4,1)S(1)} %copy.31, f32[256,8]{0,1:T(8,128)S(1)} %bitcast.292), kind=kOutput, calls=%fused_computation.144 | convolution fusion | flops 2189950976 | bytes 43532288 | tf_op jit(solution)/shard_map/hts,shd->htd/dot_general | solution.py:156
  (77 shorter events, 17.4 us)
Async XLA Ops:
  7.2 572.8 %copy-start = (bf16[256,1024]{1,0:T(8,128)(2,1)S(1)}, bf16[256,1024]{1,0:T(8,128)(2,1)}, u32[]{:S(2)}) copy-start(bf16[256,1024]{1,0:T(8,128)(2,1)} %param.17) | copy-start | bytes 1572868
  7.2 246.4 %all-gather.4.cloned.1.call-start = ((), (), s32[]{:S(2)}) async-start(), calls=%async_computation | async-start | bytes 4456448 | tf_op jit(solution)/shard_map/all_gather | solution.py:173
  23.4 556.6 %all-gather.6.cloned.1.call-start = ((), (), s32[]{:S(2)}) async-start(), calls=%async_computation.1 | async-start | bytes 8912896 | tf_op jit(solution)/shard_map/all_gather | solution.py:136
  27.2 17.8 %collective-permute-start = (bf16[256,1024]{0,1:T(8,128)(2,1)S(1)}, bf16[256,1024]{0,1:T(8,128)(2,1)S(1)}, u32[]{:S(2)}, u32[]{:S(2)}) collective-permute-start(bf16[256,1024]{0,1:T(8,128)(2,1)S(1)} %get-tuple-element.34), channel_id=1, source_target_pairs={{0,64},{8,72},{16,80},{24,88},{32,96},{40,104},{48,112},{56,120},{... | collective-permute-start | bytes 1572872 | tf_op jit(solution)/shard_map/ppermute | solution.py:15
  30.5 14.7 %copy-start.7 = (f32[1,256,1024]{1,2,0:T(8,128)S(1)}, f32[1,256,1024]{1,2,0:T(8,128)}, u32[]{:S(2)}) copy-start(f32[1,256,1024]{1,2,0:T(8,128)} %get-tuple-element.33) | copy-start | bytes 3145732
  49.0 64.4 %collective-permute-start.1 = (bf16[2,2,256,1024]{2,3,1,0:T(8,128)(2,1)}, bf16[2,2,256,1024]{2,3,1,0:T(8,128)(2,1)}, u32[]{:S(2)}, u32[]{:S(2)}) collective-permute-start(bf16[2,2,256,1024]{2,3,1,0:T(8,128)(2,1)} %pad_maximum_fusion.2), channel_id=1, source_target_pairs={{0,32},{8,40},{16,48},{24,56},{32,0},{40,8},{48,16},{56,24},{64,96... | collective-permute-start | bytes 6291464 | tf_op jit(solution)/shard_map/ppermute | solution.py:15
  118.9 48.0 %collective-permute-start.2 = (bf16[2,2,256,1024]{2,3,1,0:T(8,128)(2,1)S(1)}, bf16[2,2,256,1024]{2,3,1,0:T(8,128)(2,1)}, u32[]{:S(2)}, u32[]{:S(2)}) collective-permute-start(bf16[2,2,256,1024]{2,3,1,0:T(8,128)(2,1)S(1)} %pad_maximum_fusion.3), channel_id=1, source_target_pairs={{0,16},{8,24},{16,0},{24,8},{32,48},{40,56},{48,32},{56,40},{64,80... | collective-permute-start | bytes 6291464 | tf_op jit(solution)/shard_map/ppermute | solution.py:15
  172.2 3.9 copy-start.9
  173.7 65.4 %collective-permute-start.3 = (bf16[2,2,256,1024]{2,3,1,0:T(8,128)(2,1)}, bf16[2,2,256,1024]{2,3,1,0:T(8,128)(2,1)}, u32[]{:S(2)}, u32[]{:S(2)}) collective-permute-start(bf16[2,2,256,1024]{2,3,1,0:T(8,128)(2,1)} %pad_maximum_fusion.4), channel_id=1, source_target_pairs={{0,8},{8,0},{16,24},{24,16},{32,40},{40,32},{48,56},{56,48},{64,72... | collective-permute-start | bytes 6291464 | tf_op jit(solution)/shard_map/ppermute | solution.py:15
  175.8 475.8 %all-gather.8.cloned.1.call-start = ((), (), s32[]{:S(2)}) async-start(), calls=%async_computation.2 | async-start | bytes 8912896 | tf_op jit(solution)/shard_map/all_gather | solution.py:137
  242.3 2.9 copy-start.1
  374.5 3.2 copy-start.2
  396.1 1.4 copy-start.3
  399.1 39.0 %collective-permute-start.4 = (bf16[2,2,256,1024]{2,3,1,0:T(8,128)(2,1)}, bf16[2,2,256,1024]{2,3,1,0:T(8,128)(2,1)}, u32[]{:S(2)}, u32[]{:S(2)}) collective-permute-start(bf16[2,2,256,1024]{2,3,1,0:T(8,128)(2,1)} %pad_maximum_fusion.5), channel_id=1, source_target_pairs={{0,8},{8,0},{16,24},{24,16},{32,40},{40,32},{48,56},{56,48},{64,72... | collective-permute-start | bytes 6291464 | tf_op jit(solution)/shard_map/ppermute | solution.py:15
  443.6 40.6 %copy-start.5 = (f32[2,256,1024]{1,2,0:T(8,128)S(1)}, f32[2,256,1024]{1,2,0:T(8,128)}, u32[]{:S(2)}) copy-start(f32[2,256,1024]{1,2,0:T(8,128)} %get-tuple-element.18) | copy-start | bytes 6291460
  445.2 39.1 %collective-permute-start.5 = (bf16[2,2,256,1024]{2,3,1,0:T(8,128)(2,1)}, bf16[2,2,256,1024]{2,3,1,0:T(8,128)(2,1)}, u32[]{:S(2)}, u32[]{:S(2)}) collective-permute-start(bf16[2,2,256,1024]{2,3,1,0:T(8,128)(2,1)} %pad_maximum_fusion.6), channel_id=1, source_target_pairs={{0,16},{8,24},{16,0},{24,8},{32,48},{40,56},{48,32},{56,40},{64,80... | collective-permute-start | bytes 6291464 | tf_op jit(solution)/shard_map/ppermute | solution.py:15
  489.8 39.9 %collective-permute-start.6 = (bf16[2,2,256,1024]{2,3,1,0:T(8,128)(2,1)S(1)}, bf16[2,2,256,1024]{2,3,1,0:T(8,128)(2,1)}, u32[]{:S(2)}, u32[]{:S(2)}) collective-permute-start(bf16[2,2,256,1024]{2,3,1,0:T(8,128)(2,1)S(1)} %pad_maximum_fusion.7), channel_id=1, source_target_pairs={{0,32},{8,40},{16,48},{24,56},{32,0},{40,8},{48,16},{56,24},{64,96... | collective-permute-start | bytes 6291464 | tf_op jit(solution)/shard_map/ppermute | solution.py:15
  536.7 34.0 %collective-permute-start.7 = (bf16[2,2,256,1024]{2,3,1,0:T(8,128)(2,1)}, bf16[2,2,256,1024]{2,3,1,0:T(8,128)(2,1)}, u32[]{:S(2)}, u32[]{:S(2)}) collective-permute-start(bf16[2,2,256,1024]{2,3,1,0:T(8,128)(2,1)} %pad_maximum_fusion.8), channel_id=1, source_target_pairs={{0,64},{8,72},{16,80},{24,88},{32,96},{40,104},{48,112},{56,120},{... | collective-permute-start | bytes 6291464 | tf_op jit(solution)/shard_map/ppermute | solution.py:15
  538.7 33.4 %copy-start.4 = (f32[2,256,1024]{1,2,0:T(8,128)S(1)}, f32[2,256,1024]{1,2,0:T(8,128)}, u32[]{:S(2)}) copy-start(f32[2,256,1024]{1,2,0:T(8,128)} %get-tuple-element.10) | copy-start | bytes 6291460
  572.1 2.4 copy-start.8
  572.1 2.4 copy-start.10
  574.5 1.5 copy-start.11
  598.4 16.4 %copy-start.6 = (bf16[256,1024]{0,1:T(8,128)(2,1)S(1)}, bf16[256,1024]{0,1:T(8,128)(2,1)}, u32[]{:S(2)}) copy-start(bf16[256,1024]{0,1:T(8,128)(2,1)} %fusion.57) | copy-start | bytes 1572868
Sparse Core Ops, SparseCore 0:
  23.5 73.5 all-gather.3
  175.9 90.3 all-gather.5
  576.1 75.4 all-gather.7
where the time goes:
time: 682 us; the launch traced here: 676 us
  waiting for transfers between devices  370 us (54%)
  matrix products  163 us (24%)
  other arithmetic  69.2 us (10%)
  local copies, waits for them, and re-layouts  35.3 us (5%)
  blocking collectives  15.2 us (2%)
  between operations  14.6 us (2%)
  starting transfers between devices  8.07 us (1%)
    ppermute x8, waiting for transfers between devices, swapped(): return lax.ppermute(value, axis, pairs)  335 us
    dot_general x1, matrix products, butterfly_conv(): table_im = -jnp.dot(bank, jnp.sin(angles), precision=highest)  49.3 us
    dot_general x1, matrix products, butterfly_conv(): table_re = jnp.dot(bank, jnp.cos(angles), precision=highest)  48.3 us
    another operation x15, other arithmetic, butterfly_conv(): received = swapped(shortened(jnp.stack(state)), 'seq', level)  37.4 us
    all_gather x1, waiting for transfers between devices, attention(): value_piece = lax.all_gather(hyena_out, 'seq', axis=0, tiled=True)  35.7 us
    dot_general x8, matrix products, apply_matrix(): return jnp.einsum('km,emc->ekc', matrix, data, precision=highest)  29.4 us
    dot_general x1, matrix products, attention(): jnp.einsum('thd,shd->hts', queries, keys_here, preferred_element_type=jnp...  18.4 us
    reduce_sum x1, other arithmetic, attention(): new_total = jnp.sum(weights, axis=-1)  16.4 us
  transfers between devices with their start and end apart: 11, of which 9 were waited for; matrix products, arithmetic and copies ran while one was open for 37% of the time, Pallas kernels for 0%

commit v1 on v0

--- a/solution.py
+++ b/solution.py
@@ -134,7 +134,24 @@
     query_pos = device * rows_dev + jnp.arange(rows_dev, dtype=jnp.int32)
     scale = HD ** (-0.5)
     key_piece = lax.all_gather(att_keys, "seq", axis=0, tiled=True)
-    value_piece = lax.all_gather(hyena_out, "seq", axis=0, tiled=True)
+    size, index_2, rows = (lax.axis_size("seq"), lax.axis_index("seq"), hyena_out.shape[0])
+    ahead = [(i, (i + 1) % size) for i in range(size)]
+    downward = [(i, (i - 1) % size) for i in range(size)]
+    out = jnp.zeros((*hyena_out.shape[:0], size * rows, *hyena_out.shape[0 + 1 :]), hyena_out.dtype)
+    out = lax.dynamic_update_slice_in_dim(out, hyena_out, index_2 * rows, axis=0)
+    from_left = from_right = hyena_out
+    half = size // 2
+    for step in range(1, half + 1):
+        from_left = lax.ppermute(from_left, "seq", ahead)
+        out = lax.dynamic_update_slice_in_dim(
+            out, from_left, (index_2 - step) % size * rows, axis=0
+        )
+        if step < size - half:
+            from_right = lax.ppermute(from_right, "seq", downward)
+            out = lax.dynamic_update_slice_in_dim(
+                out, from_right, (index_2 + step) % size * rows, axis=0
+            )
+    value_piece = out
     piece_rows = key_piece.shape[0]
     key_pos = jnp.arange(piece_rows, dtype=jnp.int32)
     onehot = (

time: 682 us -> 757 us (1.11)
  starting transfers between devices: 8.07 us -> 48 us
  local copies, waits for them, and re-layouts: 35.3 us -> 60.8 us
  waiting for transfers between devices: 370 us -> 381 us
    ppermute x0 -> x15, waiting for transfers between devices: none -> 46.1 us  [the longest x8 44.7 us: attention(): from_left = lax.ppermute(from_left, 'seq', ahead)]
    ppermute x0 -> x15, starting transfers between devices: none -> 40 us  [the longest x7 37 us: attention(): from_right = lax.ppermute(from_right, 'seq', downward)]
    all_gather x1 -> x0, waiting for transfers between devices: 35.7 us -> none  [attention(): value_piece = lax.all_gather(hyena_out, 'seq', axis=0, tiled=True)]
    dynamic_update_slice x0 -> x15, local copies, waits for them, and re-layouts: none -> 21.4 us  [the longest x7 11.3 us: attention(): lax.dynamic_update_slice_in_dim(out, from_right, (index_2 + step) % size...]
  transfers between devices with their start and end apart: 11 -> 25, of which waited for: 9 -> 15; matrix products, arithmetic and copies ran while one was open for 37% -> 36% of each run, Pallas kernels for 0% -> 0%
where the time goes in v1:
time: 757 us; the launch traced here: 750 us
  waiting for transfers between devices  381 us (50%)
  matrix products  163 us (22%)
  other arithmetic  68 us (9%)
  local copies, waits for them, and re-layouts  60.8 us (8%)
  starting transfers between devices  48 us (6%)
  blocking collectives  15.2 us (2%)
  between operations  14.8 us (2%)
    ppermute x8, waiting for transfers between devices, swapped(): return lax.ppermute(value, axis, pairs)  335 us
    dot_general x1, matrix products, butterfly_conv(): table_im = -jnp.dot(bank, jnp.sin(angles), precision=highest)  49.3 us
    dot_general x1, matrix products, butterfly_conv(): table_re = jnp.dot(bank, jnp.cos(angles), precision=highest)  48.3 us
    ppermute x8, waiting for transfers between devices, attention(): from_left = lax.ppermute(from_left, 'seq', ahead)  44.7 us
    another operation x15, other arithmetic, butterfly_conv(): received = swapped(shortened(jnp.stack(state)), 'seq', level)  37.2 us
    ppermute x7, starting transfers between devices, attention(): from_right = lax.ppermute(from_right, 'seq', downward)  37 us
    dot_general x8, matrix products, apply_matrix(): return jnp.einsum('km,emc->ekc', matrix, data, precision=highest)  29.4 us
    dot_general x1, matrix products, attention(): jnp.einsum('thd,shd->hts', queries, keys_here, preferred_element_type=jnp...  18.2 us
  transfers between devices with their start and end apart: 25, of which 15 were waited for; matrix products, arithmetic and copies ran while one was open for 36% of the time, Pallas kernels for 0%

profile of v1, /device:TPU:0, one launch (start us, length us, event | category | flops | bytes accessed | tf_op | source)
XLA Modules:
  0.0 750.3 jit_solution(195048385253374852)
XLA Ops:
  8.1 15.2 %all_gather.9 = bf16[512,256]{1,0:T(8,128)(2,1)} all-gather(bf16[64,256]{1,0:T(8,128)(2,1)S(1)} %convert_element_type.294), channel_id=1, replica_groups=mesh['seq'=16,'chan'=8] {'chan'}, dimensions={0}, use_global_device_ids=true | all-gather | bytes 294912 | tf_op jit(solution)/shard_map/all_gather | solution.py:187
  27.2 3.0 collective-permute-start
  30.5 14.4 %collective-permute-done = bf16[256,1024]{0,1:T(8,128)(2,1)S(1)} collective-permute-done((bf16[256,1024]{0,1:T(8,128)(2,1)S(1)}, bf16[256,1024]{0,1:T(8,128)(2,1)S(1)}, u32[]{:S(2)}, u32[]{:S(2)}) %collective-permute-start) | collective-permute-done | bytes 524320 | tf_op jit(solution)/shard_map/ppermute | solution.py:15
  50.9 62.4 %collective-permute-done.1 = bf16[2,2,256,1024]{2,3,1,0:T(8,128)(2,1)} collective-permute-done((bf16[2,2,256,1024]{2,3,1,0:T(8,128)(2,1)}, bf16[2,2,256,1024]{2,3,1,0:T(8,128)(2,1)}, u32[]{:S(2)}, u32[]{:S(2)}) %collective-permute-start.1) | collective-permute-done | bytes 2097184 | tf_op jit(solution)/shard_map/ppermute | solution.py:15
  113.3 5.3 convert_bitcast_fusion.10
  121.6 45.3 %collective-permute-done.2 = bf16[2,2,256,1024]{2,3,1,0:T(8,128)(2,1)} collective-permute-done((bf16[2,2,256,1024]{2,3,1,0:T(8,128)(2,1)S(1)}, bf16[2,2,256,1024]{2,3,1,0:T(8,128)(2,1)}, u32[]{:S(2)}, u32[]{:S(2)}) %collective-permute-start.2) | collective-permute-done | bytes 2097184 | tf_op jit(solution)/shard_map/ppermute | solution.py:15
  166.9 5.3 convert_bitcast_fusion.8
  176.0 63.1 %collective-permute-done.3 = bf16[2,2,256,1024]{2,3,1,0:T(8,128)(2,1)} collective-permute-done((bf16[2,2,256,1024]{2,3,1,0:T(8,128)(2,1)}, bf16[2,2,256,1024]{2,3,1,0:T(8,128)(2,1)}, u32[]{:S(2)}, u32[]{:S(2)}) %collective-permute-start.3) | collective-permute-done | bytes 2097184 | tf_op jit(solution)/shard_map/ppermute | solution.py:15
  239.1 3.2 fusion.26
  242.4 2.8 fusion.84
  245.2 4.2 fusion.82
  249.4 4.2 convolution_subtract_fusion.1
  253.6 48.3 %fusion.37 = f32[512,512]{0,1:T(8,128)S(1)} fusion(bf16[512,4096]{1,0:T(8,128)(2,1)} %all-gather.3.cloned.1.call-done, s32[512]{0:T(512)S(1)} %pad_add_fusion.1), kind=kOutput, calls=%fused_computation.100 | convolution fusion | flops 12914262016 | bytes 5244928 | tf_op jit(solution)/shard_map/dot_general | solution.py:111
  302.3 49.3 %fusion.46 = f32[512,512]{0,1:T(8,128)} fusion(bf16[512,4096]{1,0:T(8,128)(2,1)} %all-gather.3.cloned.1.call-done, s32[512]{0:T(512)S(1)} %pad_add_fusion.1), kind=kOutput, calls=%fused_computation.103 | convolution fusion | flops 12914524160 | bytes 5244928 | tf_op jit(solution)/shard_map/dot_general | solution.py:112
  353.1 4.9 gather_fusion.1
  358.0 4.9 gather_fusion
  363.0 4.0 select_bitcast_fusion
  367.0 2.9 copy.27
  369.9 2.9 copy.28
  374.7 3.2 copy.25
  378.0 6.5 fusion.34
  384.5 2.8 fusion.86
  387.4 2.9 convolution_add_fusion
  390.3 2.8 fusion.88
  393.2 3.1 convolution_subtract_fusion
  399.4 39.1 %collective-permute-done.4 = bf16[2,2,256,1024]{2,3,1,0:T(8,128)(2,1)} collective-permute-done((bf16[2,2,256,1024]{2,3,1,0:T(8,128)(2,1)}, bf16[2,2,256,1024]{2,3,1,0:T(8,128)(2,1)}, u32[]{:S(2)}, u32[]{:S(2)}) %collective-permute-start.4) | collective-permute-done | bytes 2097184 | tf_op jit(solution)/shard_map/ppermute | solution.py:15
  438.4 5.4 convert_bitcast_fusion.7
  445.5 38.9 %collective-permute-done.5 = bf16[2,2,256,1024]{2,3,1,0:T(8,128)(2,1)} collective-permute-done((bf16[2,2,256,1024]{2,3,1,0:T(8,128)(2,1)}, bf16[2,2,256,1024]{2,3,1,0:T(8,128)(2,1)}, u32[]{:S(2)}, u32[]{:S(2)}) %collective-permute-start.5) | collective-permute-done | bytes 2097184 | tf_op jit(solution)/shard_map/ppermute | solution.py:15
  484.4 5.4 convert_bitcast_fusion.5
  490.1 39.8 %collective-permute-done.6 = bf16[2,2,256,1024]{2,3,1,0:T(8,128)(2,1)} collective-permute-done((bf16[2,2,256,1024]{2,3,1,0:T(8,128)(2,1)S(1)}, bf16[2,2,256,1024]{2,3,1,0:T(8,128)(2,1)}, u32[]{:S(2)}, u32[]{:S(2)}) %collective-permute-start.6) | collective-permute-done | bytes 2097184 | tf_op jit(solution)/shard_map/ppermute | solution.py:15
  530.0 5.3 convert_bitcast_fusion.2
  538.9 31.6 %collective-permute-done.7 = bf16[2,2,256,1024]{2,3,1,0:T(8,128)(2,1)} collective-permute-done((bf16[2,2,256,1024]{2,3,1,0:T(8,128)(2,1)}, bf16[2,2,256,1024]{2,3,1,0:T(8,128)(2,1)}, u32[]{:S(2)}, u32[]{:S(2)}) %collective-permute-start.7) | collective-permute-done | bytes 2097184 | tf_op jit(solution)/shard_map/ppermute | solution.py:15
  576.0 3.3 copy-done.4
  581.9 3.7 collective-permute-start.9
  585.6 11.2 %collective-permute-done.8 = bf16[256,1024]{0,1:T(8,128)(2,1)S(1)} collective-permute-done((bf16[256,1024]{0,1:T(8,128)(2,1)S(1)}, bf16[256,1024]{0,1:T(8,128)(2,1)S(1)}, u32[]{:S(2)}, u32[]{:S(2)}) %collective-permute-start.8) | collective-permute-done | bytes 524320 | tf_op jit(solution)/shard_map/ppermute | solution.py:145
  597.8 5.8 collective-permute-start.11
  603.6 10.9 %collective-permute-done.10 = bf16[256,1024]{0,1:T(8,128)(2,1)S(1)} collective-permute-done((bf16[256,1024]{0,1:T(8,128)(2,1)S(1)}, bf16[256,1024]{0,1:T(8,128)(2,1)S(1)}, u32[]{:S(2)}, u32[]{:S(2)}) %collective-permute-start.10) | collective-permute-done | bytes 524320 | tf_op jit(solution)/shard_map/ppermute | solution.py:145
  615.3 5.9 collective-permute-start.13
  621.2 9.8 %collective-permute-done.12 = bf16[256,1024]{0,1:T(8,128)(2,1)S(1)} collective-permute-done((bf16[256,1024]{0,1:T(8,128)(2,1)S(1)}, bf16[256,1024]{0,1:T(8,128)(2,1)S(1)}, u32[]{:S(2)}, u32[]{:S(2)}) %collective-permute-start.12) | collective-permute-done | bytes 524320 | tf_op jit(solution)/shard_map/ppermute | solution.py:145
  634.9 5.4 collective-permute-start.15
  640.3 6.7 collective-permute-done.14
  647.0 18.2 %fusion = (f32[8,256]{1,0:T(8,128)S(1)}, f32[8,256,4096]{2,1,0:T(8,128)}) fusion(pred[256,4096]{1,0:T(8,128)(4,1)S(1)} %copy.31, bf16[4096,8,128]{0,2,1:T(8,128)(2,1)} %bitcast.290, bf16[256,1024]{1,0:T(8,128)(2,1)S(1)} %copy-done), kind=kOutput, calls=%fused_computation.4 | convolution fusion | flops 2172647424 | bytes 43524096 | tf_op jit(solution)/shard_map/thd,shd->hts/dot_general | solution.py:166
  665.2 5.3 collective-permute-start.17
  670.5 16.2 %fusion.1 = f32[8,256]{1,0:T(8,128)S(1)} fusion(f32[8,256,4096]{2,1,0:T(8,128)} %get-tuple-element.59, f32[8,256]{1,0:T(8,128)S(1)} %broadcast_maximum_fusion, pred[256,4096]{1,0:T(8,128)(4,1)S(1)} %copy.31), kind=kLoop, calls=%fused_computation.5 | loop fusion | flops 41940992 | bytes 34619392 | tf_op jit(solution)/shard_map/reduce_sum | solution.py:172
  691.4 5.3 collective-permute-start.19
  705.1 5.5 collective-permute-start.21
  719.1 6.0 collective-permute-done.22
  726.0 16.3 %divide_convert_fusion = bf16[256,8,128]{0,2,1:T(8,128)(2,1)S(1)} fusion(bf16[4096,8,128]{0,2,1:T(8,128)(2,1)} %bitcast.291, f32[8,256,4096]{2,1,0:T(8,128)} %get-tuple-element.59, f32[8,256]{1,0:T(8,128)S(1)} %broadcast_maximum_fusion, pred[256,4096]{1,0:T(8,128)(4,1)S(1)} %copy.31, f32[256,8]{0,1:T(8,128)S(1)} %bitcast.296), kind=kOutput, calls=%fused_computation.144 | convolution fusion | flops 2189950976 | bytes 43532288 | tf_op jit(solution)/shard_map/hts,shd->htd/dot_general | solution.py:173
  (134 shorter events, 67.1 us)
Async XLA Ops:
  7.2 639.8 %copy-start = (bf16[256,1024]{1,0:T(8,128)(2,1)S(1)}, bf16[256,1024]{1,0:T(8,128)(2,1)}, u32[]{:S(2)}) copy-start(bf16[256,1024]{1,0:T(8,128)(2,1)} %param.17) | copy-start | bytes 1572868
  7.2 246.4 %all-gather.3.cloned.1.call-start = ((), (), s32[]{:S(2)}) async-start(), calls=%async_computation | async-start | bytes 4456448 | tf_op jit(solution)/shard_map/all_gather | solution.py:190
  23.4 623.6 %all-gather.5.cloned.1.call-start = ((), (), s32[]{:S(2)}) async-start(), calls=%async_computation.1 | async-start | bytes 8912896 | tf_op jit(solution)/shard_map/all_gather | solution.py:136
  27.2 17.8 %collective-permute-start = (bf16[256,1024]{0,1:T(8,128)(2,1)S(1)}, bf16[256,1024]{0,1:T(8,128)(2,1)S(1)}, u32[]{:S(2)}, u32[]{:S(2)}) collective-permute-start(bf16[256,1024]{0,1:T(8,128)(2,1)S(1)} %get-tuple-element.36), channel_id=1, source_target_pairs={{0,64},{8,72},{16,80},{24,88},{32,96},{40,104},{48,112},{56,120},{... | collective-permute-start | bytes 1572872 | tf_op jit(solution)/shard_map/ppermute | solution.py:15
  30.5 14.7 %copy-start.7 = (f32[1,256,1024]{1,2,0:T(8,128)S(1)}, f32[1,256,1024]{1,2,0:T(8,128)}, u32[]{:S(2)}) copy-start(f32[1,256,1024]{1,2,0:T(8,128)} %get-tuple-element.35) | copy-start | bytes 3145732
  48.9 64.4 %collective-permute-start.1 = (bf16[2,2,256,1024]{2,3,1,0:T(8,128)(2,1)}, bf16[2,2,256,1024]{2,3,1,0:T(8,128)(2,1)}, u32[]{:S(2)}, u32[]{:S(2)}) collective-permute-start(bf16[2,2,256,1024]{2,3,1,0:T(8,128)(2,1)} %pad_maximum_fusion.2), channel_id=1, source_target_pairs={{0,32},{8,40},{16,48},{24,56},{32,0},{40,8},{48,16},{56,24},{64,96... | collective-permute-start | bytes 6291464 | tf_op jit(solution)/shard_map/ppermute | solution.py:15
  118.9 48.0 %collective-permute-start.2 = (bf16[2,2,256,1024]{2,3,1,0:T(8,128)(2,1)S(1)}, bf16[2,2,256,1024]{2,3,1,0:T(8,128)(2,1)}, u32[]{:S(2)}, u32[]{:S(2)}) collective-permute-start(bf16[2,2,256,1024]{2,3,1,0:T(8,128)(2,1)S(1)} %pad_maximum_fusion.3), channel_id=1, source_target_pairs={{0,16},{8,24},{16,0},{24,8},{32,48},{40,56},{48,32},{56,40},{64,80... | collective-permute-start | bytes 6291464 | tf_op jit(solution)/shard_map/ppermute | solution.py:15
  172.1 3.8 copy-start.16
  173.7 65.5 %collective-permute-start.3 = (bf16[2,2,256,1024]{2,3,1,0:T(8,128)(2,1)}, bf16[2,2,256,1024]{2,3,1,0:T(8,128)(2,1)}, u32[]{:S(2)}, u32[]{:S(2)}) collective-permute-start(bf16[2,2,256,1024]{2,3,1,0:T(8,128)(2,1)} %pad_maximum_fusion.4), channel_id=1, source_target_pairs={{0,8},{8,0},{16,24},{24,16},{32,40},{40,32},{48,56},{56,48},{64,72... | collective-permute-start | bytes 6291464 | tf_op jit(solution)/shard_map/ppermute | solution.py:15
  242.4 2.9 copy-start.1
  374.7 3.2 copy-start.2
  396.3 1.4 copy-start.3
  399.3 39.1 %collective-permute-start.4 = (bf16[2,2,256,1024]{2,3,1,0:T(8,128)(2,1)}, bf16[2,2,256,1024]{2,3,1,0:T(8,128)(2,1)}, u32[]{:S(2)}, u32[]{:S(2)}) collective-permute-start(bf16[2,2,256,1024]{2,3,1,0:T(8,128)(2,1)} %pad_maximum_fusion.5), channel_id=1, source_target_pairs={{0,8},{8,0},{16,24},{24,16},{32,40},{40,32},{48,56},{56,48},{64,72... | collective-permute-start | bytes 6291464 | tf_op jit(solution)/shard_map/ppermute | solution.py:15
  443.9 40.5 %copy-start.6 = (f32[2,256,1024]{1,2,0:T(8,128)S(1)}, f32[2,256,1024]{1,2,0:T(8,128)}, u32[]{:S(2)}) copy-start(f32[2,256,1024]{1,2,0:T(8,128)} %get-tuple-element.20) | copy-start | bytes 6291460
  445.4 38.9 %collective-permute-start.5 = (bf16[2,2,256,1024]{2,3,1,0:T(8,128)(2,1)}, bf16[2,2,256,1024]{2,3,1,0:T(8,128)(2,1)}, u32[]{:S(2)}, u32[]{:S(2)}) collective-permute-start(bf16[2,2,256,1024]{2,3,1,0:T(8,128)(2,1)} %pad_maximum_fusion.6), channel_id=1, source_target_pairs={{0,16},{8,24},{16,0},{24,8},{32,48},{40,56},{48,32},{56,40},{64,80... | collective-permute-start | bytes 6291464 | tf_op jit(solution)/shard_map/ppermute | solution.py:15
  490.0 40.0 %collective-permute-start.6 = (bf16[2,2,256,1024]{2,3,1,0:T(8,128)(2,1)S(1)}, bf16[2,2,256,1024]{2,3,1,0:T(8,128)(2,1)}, u32[]{:S(2)}, u32[]{:S(2)}) collective-permute-start(bf16[2,2,256,1024]{2,3,1,0:T(8,128)(2,1)S(1)} %pad_maximum_fusion.7), channel_id=1, source_target_pairs={{0,32},{8,40},{16,48},{24,56},{32,0},{40,8},{48,16},{56,24},{64,96... | collective-permute-start | bytes 6291464 | tf_op jit(solution)/shard_map/ppermute | solution.py:15
  536.8 33.7 %collective-permute-start.7 = (bf16[2,2,256,1024]{2,3,1,0:T(8,128)(2,1)}, bf16[2,2,256,1024]{2,3,1,0:T(8,128)(2,1)}, u32[]{:S(2)}, u32[]{:S(2)}) collective-permute-start(bf16[2,2,256,1024]{2,3,1,0:T(8,128)(2,1)} %pad_maximum_fusion.8), channel_id=1, source_target_pairs={{0,64},{8,72},{16,80},{24,88},{32,96},{40,104},{48,112},{56,120},{... | collective-permute-start | bytes 6291464 | tf_op jit(solution)/shard_map/ppermute | solution.py:15
  538.8 33.0 %copy-start.5 = (f32[2,256,1024]{1,2,0:T(8,128)S(1)}, f32[2,256,1024]{1,2,0:T(8,128)}, u32[]{:S(2)}) copy-start(f32[2,256,1024]{1,2,0:T(8,128)} %get-tuple-element.40) | copy-start | bytes 6291460
  574.2 1.1 copy-start.10
  574.2 1.1 copy-start.17
  575.3 39.2 %copy-start.18 = (s32[2,32]{1,0:T(2,128)S(1)}, s32[2,32]{1,0:T(2,128)}, u32[]{:S(2)}) copy-start(s32[2,32]{1,0:T(2,128)} %param.19) | copy-start | bytes 772
  576.0 3.3 copy-start.4
  579.3 2.6 copy-start.8
  579.3 17.6 %collective-permute-start.8 = (bf16[256,1024]{0,1:T(8,128)(2,1)S(1)}, bf16[256,1024]{0,1:T(8,128)(2,1)S(1)}, u32[]{:S(2)}, u32[]{:S(2)}) collective-permute-start(bf16[256,1024]{0,1:T(8,128)(2,1)S(1)} %get-tuple-element.8), channel_id=1, source_target_pairs={{0,8},{8,16},{16,24},{24,32},{32,40},{40,48},{48,56},{56,64},{64,7... | collective-permute-start | bytes 1572872 | tf_op jit(solution)/shard_map/ppermute | solution.py:145
  581.9 15.9 %collective-permute-start.9 = (bf16[256,1024]{0,1:T(8,128)(2,1)S(1)}, bf16[256,1024]{0,1:T(8,128)(2,1)S(1)}, u32[]{:S(2)}, u32[]{:S(2)}) collective-permute-start(bf16[256,1024]{0,1:T(8,128)(2,1)S(1)} %get-tuple-element.8), channel_id=1, source_target_pairs={{0,120},{8,0},{16,8},{24,16},{32,24},{40,32},{48,40},{56,48},{64,5... | collective-permute-start | bytes 1572872 | tf_op jit(solution)/shard_map/ppermute | solution.py:150
  596.8 6.8 copy-start.11
  596.8 17.7 %collective-permute-start.10 = (bf16[256,1024]{0,1:T(8,128)(2,1)S(1)}, bf16[256,1024]{0,1:T(8,128)(2,1)S(1)}, u32[]{:S(2)}, u32[]{:S(2)}) collective-permute-start(bf16[256,1024]{0,1:T(8,128)(2,1)S(1)} %collective-permute-done.8), channel_id=1, source_target_pairs={{0,8},{8,16},{16,24},{24,32},{32,40},{40,48},{48,56},{56,64},{64,7... | collective-permute-start | bytes 1572872 | tf_op jit(solution)/shard_map/ppermute | solution.py:145
  597.8 33.2 %copy-start.13 = (bf16[256,1024]{0,1:T(8,128)(2,1)}, bf16[256,1024]{0,1:T(8,128)(2,1)S(1)}, u32[]{:S(2)}) copy-start(bf16[256,1024]{0,1:T(8,128)(2,1)S(1)} %collective-permute-done.9) | copy-start | bytes 1572868
  597.8 17.5 %collective-permute-start.11 = (bf16[256,1024]{0,1:T(8,128)(2,1)S(1)}, bf16[256,1024]{0,1:T(8,128)(2,1)}, u32[]{:S(2)}, u32[]{:S(2)}) collective-permute-start(bf16[256,1024]{0,1:T(8,128)(2,1)S(1)} %collective-permute-done.9), channel_id=1, source_target_pairs={{0,120},{8,0},{16,8},{24,16},{32,24},{40,32},{48,40},{56,48},{64,5... | collective-permute-start | bytes 1572872 | tf_op jit(solution)/shard_map/ppermute | solution.py:150
  614.6 16.5 %copy-start.14 = (bf16[256,1024]{0,1:T(8,128)(2,1)}, bf16[256,1024]{0,1:T(8,128)(2,1)S(1)}, u32[]{:S(2)}) copy-start(bf16[256,1024]{0,1:T(8,128)(2,1)S(1)} %collective-permute-done.10) | copy-start | bytes 1572868
  614.6 16.5 %collective-permute-start.12 = (bf16[256,1024]{0,1:T(8,128)(2,1)S(1)}, bf16[256,1024]{0,1:T(8,128)(2,1)S(1)}, u32[]{:S(2)}, u32[]{:S(2)}) collective-permute-start(bf16[256,1024]{0,1:T(8,128)(2,1)S(1)} %collective-permute-done.10), channel_id=1, source_target_pairs={{0,8},{8,16},{16,24},{24,32},{32,40},{40,48},{48,56},{56,64},{64,7... | collective-permute-start | bytes 1572872 | tf_op jit(solution)/shard_map/ppermute | solution.py:145
  615.3 19.5 %collective-permute-start.13 = (bf16[256,1024]{0,1:T(8,128)(2,1)}, bf16[256,1024]{0,1:T(8,128)(2,1)}, u32[]{:S(2)}, u32[]{:S(2)}) collective-permute-start(bf16[256,1024]{0,1:T(8,128)(2,1)} %collective-permute-done.11), channel_id=1, source_target_pairs={{0,120},{8,0},{16,8},{24,16},{32,24},{40,32},{48,40},{56,48},{64,5... | collective-permute-start | bytes 1572872 | tf_op jit(solution)/shard_map/ppermute | solution.py:150
  631.0 15.9 %collective-permute-start.14 = (bf16[256,1024]{0,1:T(8,128)(2,1)S(1)}, bf16[256,1024]{0,1:T(8,128)(2,1)}, u32[]{:S(2)}, u32[]{:S(2)}) collective-permute-start(bf16[256,1024]{0,1:T(8,128)(2,1)S(1)} %collective-permute-done.12), channel_id=1, source_target_pairs={{0,8},{8,16},{16,24},{24,32},{32,40},{40,48},{48,56},{56,64},{64,7... | collective-permute-start | bytes 1572872 | tf_op jit(solution)/shard_map/ppermute | solution.py:145
  634.9 30.3 %collective-permute-start.15 = (bf16[256,1024]{0,1:T(8,128)(2,1)}, bf16[256,1024]{0,1:T(8,128)(2,1)}, u32[]{:S(2)}, u32[]{:S(2)}) collective-permute-start(bf16[256,1024]{0,1:T(8,128)(2,1)} %collective-permute-done.13), channel_id=1, source_target_pairs={{0,120},{8,0},{16,8},{24,16},{32,24},{40,32},{48,40},{56,48},{64,5... | collective-permute-start | bytes 1572872 | tf_op jit(solution)/shard_map/ppermute | solution.py:150
  647.0 23.5 %collective-permute-start.16 = (bf16[256,1024]{0,1:T(8,128)(2,1)}, bf16[256,1024]{0,1:T(8,128)(2,1)}, u32[]{:S(2)}, u32[]{:S(2)}) collective-permute-start(bf16[256,1024]{0,1:T(8,128)(2,1)} %collective-permute-done.14), channel_id=1, source_target_pairs={{0,8},{8,16},{16,24},{24,32},{32,40},{40,48},{48,56},{56,64},{64,7... | collective-permute-start | bytes 1572872 | tf_op jit(solution)/shard_map/ppermute | solution.py:145
  665.2 26.2 %collective-permute-start.17 = (bf16[256,1024]{0,1:T(8,128)(2,1)}, bf16[256,1024]{0,1:T(8,128)(2,1)}, u32[]{:S(2)}, u32[]{:S(2)}) collective-permute-start(bf16[256,1024]{0,1:T(8,128)(2,1)} %collective-permute-done.15), channel_id=1, source_target_pairs={{0,120},{8,0},{16,8},{24,16},{32,24},{40,32},{48,40},{56,48},{64,5... | collective-permute-start | bytes 1572872 | tf_op jit(solution)/shard_map/ppermute | solution.py:150
  670.5 28.1 %collective-permute-start.18 = (bf16[256,1024]{0,1:T(8,128)(2,1)}, bf16[256,1024]{0,1:T(8,128)(2,1)}, u32[]{:S(2)}, u32[]{:S(2)}) collective-permute-start(bf16[256,1024]{0,1:T(8,128)(2,1)} %collective-permute-done.16), channel_id=1, source_target_pairs={{0,8},{8,16},{16,24},{24,32},{32,40},{40,48},{48,56},{56,64},{64,7... | collective-permute-start | bytes 1572872 | tf_op jit(solution)/shard_map/ppermute | solution.py:145
  670.5 16.2 %copy-start.9 = (bf16[256,1024]{0,1:T(8,128)(2,1)S(1)}, bf16[256,1024]{0,1:T(8,128)(2,1)}, u32[]{:S(2)}) copy-start(bf16[256,1024]{0,1:T(8,128)(2,1)} %copy-done.8) | copy-start | bytes 1572868
  670.5 17.2 %copy-start.12 = (bf16[256,1024]{0,1:T(8,128)(2,1)S(1)}, bf16[256,1024]{0,1:T(8,128)(2,1)}, u32[]{:S(2)}) copy-start(bf16[256,1024]{0,1:T(8,128)(2,1)} %copy-done.11) | copy-start | bytes 1572868
  687.7 2.8 copy-start.15
  691.4 13.8 %collective-permute-start.19 = (bf16[256,1024]{0,1:T(8,128)(2,1)}, bf16[256,1024]{0,1:T(8,128)(2,1)S(1)}, u32[]{:S(2)}, u32[]{:S(2)}) collective-permute-start(bf16[256,1024]{0,1:T(8,128)(2,1)} %collective-permute-done.17), channel_id=1, source_target_pairs={{0,120},{8,0},{16,8},{24,16},{32,24},{40,32},{48,40},{56,48},{64,5... | collective-permute-start | bytes 1572872 | tf_op jit(solution)/shard_map/ppermute | solution.py:150
  698.6 14.0 %collective-permute-start.20 = (bf16[256,1024]{0,1:T(8,128)(2,1)}, bf16[256,1024]{0,1:T(8,128)(2,1)S(1)}, u32[]{:S(2)}, u32[]{:S(2)}) collective-permute-start(bf16[256,1024]{0,1:T(8,128)(2,1)} %collective-permute-done.18), channel_id=1, source_target_pairs={{0,8},{8,16},{16,24},{24,32},{32,40},{40,48},{48,56},{56,64},{64,7... | collective-permute-start | bytes 1572872 | tf_op jit(solution)/shard_map/ppermute | solution.py:145
  705.1 13.0 %collective-permute-start.21 = (bf16[256,1024]{0,1:T(8,128)(2,1)S(1)}, bf16[256,1024]{0,1:T(8,128)(2,1)S(1)}, u32[]{:S(2)}, u32[]{:S(2)}) collective-permute-start(bf16[256,1024]{0,1:T(8,128)(2,1)S(1)} %collective-permute-done.19), channel_id=1, source_target_pairs={{0,120},{8,0},{16,8},{24,16},{32,24},{40,32},{48,40},{56,48},{64,5... | collective-permute-start | bytes 1572872 | tf_op jit(solution)/shard_map/ppermute | solution.py:150
  712.6 12.5 %collective-permute-start.22 = (bf16[256,1024]{0,1:T(8,128)(2,1)S(1)}, bf16[256,1024]{0,1:T(8,128)(2,1)S(1)}, u32[]{:S(2)}, u32[]{:S(2)}) collective-permute-start(bf16[256,1024]{0,1:T(8,128)(2,1)S(1)} %collective-permute-done.20), channel_id=1, source_target_pairs={{0,8},{8,16},{16,24},{24,32},{32,40},{40,48},{48,56},{56,64},{64,7... | collective-permute-start | bytes 1572872 | tf_op jit(solution)/shard_map/ppermute | solution.py:145
Sparse Core Ops, SparseCore 0:
  23.5 73.5 all-gather.2
  176.0 90.3 all-gather.4
